TPU v7x, 768 devices: a whole 4x8x12 slice. The times are simulated.
768 devices in a mesh: blk: 96 (over y, z), grp: 8 (over x, core).
Axes of the slice: x: 4, y: 8, z: 12, core: 2. Of those that a mesh axis runs over, the one named last changes fastest.
Arguments:
- points: float32 [49152, 256], P(('blk', 'grp')), may hold values from -6 to 6
- centroids: float32 [135168, 256], P(('blk', 'grp')), may hold values from -6 to 6
- counts: float32 [135168], P(('blk', 'grp')), may hold values from 1 to 20
- assign: int32 [49152], P(('blk', 'grp')), may hold values from 0 to 1407, as said below
Outputs:
- nearest: float32 [49152], P(('blk', 'grp'))
- new_centroids: float32 [135168, 256], P(('blk', 'grp'))
- new_counts: float32 [135168], P(('blk', 'grp'))
Inputs may be any that keep to these rules, and one draw needn't show every extreme that they name: Every point of coarse cell b names a centroid of that cell. Of the 64 points of one device, at most 32 name centroids held by one device of its group along grp (owner assign // 176); every device sends exactly 32 to one owner, and in every group one owner receives 32 from each of the group's devices.
All inputs are finite; a program needn't handle non-finite values.
Results may differ from a plain program's by a relative error of at most 0.0028.
Values may be sent and summed in bfloat16 or wider, within the bound.
No kernel may reach another device: no remote copies, remote signals or barrier semaphores. Data moves between devices by JAX's collectives and lax.ppermute only.
A program may use at most 32 MiB of HBM per device.

v0:
```python
import jax
import jax.numpy as jnp
from jax import lax
from jax.sharding import PartitionSpec as P


def nearest_fold(rows_low, running, portion):
    row_norms = jnp.sum(jnp.square(portion.astype(jnp.float32)), axis=1)
    scores = lax.dot_general(
        rows_low, portion, (((1,), (1,)), ((), ())), preferred_element_type=jnp.float32
    )
    return jnp.minimum(running, jnp.min(row_norms[None, :] - 2.0 * scores, axis=1))


def on_device(points, centroids, counts, assign):
    pts_rows = points.shape[0]
    feature_width = points.shape[1]
    cen_rows = centroids.shape[0]
    groups = lax.axis_size("grp")
    points_low = points.astype(jnp.bfloat16)
    centroids_low = centroids.astype(jnp.bfloat16)
    point_norms = jnp.sum(points * points, axis=1)
    gathered = lax.all_gather(points_low, "grp", axis=0, tiled=True)
    start_min = jnp.full((gathered.shape[0],), jnp.inf, jnp.float32)
    partial_value = nearest_fold(
        gathered, start_min, lax.all_gather(centroids_low, "blk", axis=0, tiled=True)
    )
    combined = lax.pmin(partial_value, "grp")
    own_rows = lax.dynamic_slice_in_dim(combined, lax.axis_index("grp") * pts_rows, pts_rows)
    nearest = (point_norms + own_rows) / feature_width
    capacity = pts_rows // 2
    owner_index = assign // cen_rows
    local_index = assign - owner_index * cen_rows
    owner_hits = (owner_index[:, None] == jnp.arange(groups, dtype=jnp.int32)[None, :]).astype(
        jnp.int32
    )
    position = jnp.sum((jnp.cumsum(owner_hits, axis=0) - owner_hits) * owner_hits, axis=1)
    slot_index = owner_index * capacity + position
    dispatch = (
        slot_index[None, :] == jnp.arange(groups * capacity, dtype=jnp.int32)[:, None]
    ).astype(jnp.float32)
    outgoing = jnp.dot(dispatch, points, precision=lax.Precision.HIGHEST).reshape(
        groups, capacity, feature_width
    )
    slot_cell = (
        jnp.dot(dispatch, (local_index + 1).astype(jnp.float32), precision=lax.Precision.HIGHEST)
        - 1.0
    )
    incoming, incoming_cell = (
        lax.all_to_all(
            outgoing.astype(jnp.bfloat16), "grp", split_axis=0, concat_axis=0, tiled=True
        ).astype(outgoing.dtype),
        lax.all_to_all(
            slot_cell.reshape(groups, capacity).astype(jnp.bfloat16),
            "grp",
            split_axis=0,
            concat_axis=0,
            tiled=True,
        ).astype(jnp.float32),
    )
    cell_ids = incoming_cell.reshape(-1).astype(jnp.int32)
    matches = (cell_ids[None, :] == jnp.arange(cen_rows, dtype=jnp.int32)[:, None]).astype(
        jnp.float32
    )
    totals = jnp.dot(matches, incoming.reshape(-1, feature_width), precision=lax.Precision.HIGHEST)
    arrivals = jnp.sum(matches, axis=1)
    new_counts = counts + arrivals
    new_centroids = (counts[:, None] * centroids + totals) / new_counts[:, None]
    return (nearest, new_centroids, new_counts)


def solution(mesh):
    return jax.shard_map(
        on_device,
        mesh=mesh,
        in_specs=(
            P(("blk", "grp"), None),
            P(("blk", "grp"), None),
            P(("blk", "grp")),
            P(("blk", "grp")),
        ),
        out_specs=(P(("blk", "grp")), P(("blk", "grp"), None), P(("blk", "grp"))),
        check_vma=False,
    )
```

profile of v0, /device:TPU:1, one launch (start us, length us, event | category | flops | bytes accessed | tf_op | source)
XLA Modules:
  0.0 187.6 jit_solution(11988279217142007454)
XLA Ops:
  7.2 0.0 all-gather.2.cloned.1.call-start
  7.2 1.6 convert_element_type.58
  8.8 0.0 all-gather.2.cloned.1.call-update
  8.8 0.7 and_select_fusion
  9.5 0.1 fusion.5
  9.5 0.1 reduce_window_sum.11
  9.6 0.2 select_reduce_fusion
  9.8 0.7 multiply_add_fusion
  10.5 0.8 fusion.1
  11.3 0.7 convert_element_type.71
  12.0 13.7 %all-to-all-start = ((bf16[8,1,32]{2,1,0:T(2,128)(2,1)}), bf16[8,1,32]{2,1,0:T(2,128)(2,1)S(1)}, u32[]{:S(2)}, u32[]{:S(2)}) async-start(bf16[8,1,32]{2,1,0:T(2,128)(2,1)} %convert_element_type.71), calls=%async_computation | async-start | bytes 8192 | tf_op jit(solution)/shard_map/all_to_all | solution.py:53
  25.8 1.0 fusion.15
  26.8 13.5 %all_gather.7 = bf16[512,256]{1,0:T(8,128)(2,1)S(1)} all-gather(bf16[64,256]{1,0:T(8,128)(2,1)S(1)} %get-tuple-element.3), channel_id=1, replica_groups=mesh['blk'=96,'grp'=8] {'grp'}, dimensions={0}, use_global_device_ids=true | all-gather | bytes 294912 | tf_op jit(solution)/shard_map/all_gather | solution.py:23
  40.3 1.8 convolution_convert_fusion
  42.1 0.0 all-to-all-done
  42.1 3.8 %all-to-all-start.1 = ((bf16[8,32,256]{2,1,0:T(8,128)(2,1)}), bf16[8,32,256]{2,1,0:T(8,128)(2,1)S(1)}, u32[]{:S(2)}, u32[]{:S(2)}) async-start(bf16[8,32,256]{2,1,0:T(8,128)(2,1)} %bitcast.2), calls=%async_computation.1 | async-start | bytes 262144 | tf_op jit(solution)/shard_map/all_to_all | solution.py:50
  46.0 0.1 convert_element_type.67
  46.0 0.1 convert_reduce_fusion
  46.2 0.7 add.26
  46.8 0.0 copy-start.1
  46.8 4.4 %all-to-all-done.1 = bf16[8,32,256]{2,1,0:T(8,128)(2,1)S(1)} async-done(((bf16[8,32,256]{2,1,0:T(8,128)(2,1)}), bf16[8,32,256]{2,1,0:T(8,128)(2,1)S(1)}, u32[]{:S(2)}, u32[]{:S(2)}) %all-to-all-start.1) | async-done | bytes 131104 | tf_op jit(solution)/shard_map/all_to_all | solution.py:50
  51.2 1.8 fusion
  53.0 99.2 %all-gather.2.cloned.1.call-done = bf16[16896,256]{1,0:T(8,128)(2,1)} async-done(((bf16[176,256]{1,0:T(8,128)(2,1)}), bf16[16896,256]{1,0:T(8,128)(2,1)}) %all-gather.2.cloned.1.call-update) | async-done | bytes 8650768 | tf_op jit(solution)/shard_map/all_gather | solution.py:26
  152.2 0.0 copy-start
  152.2 5.8 %multiply_reduce_fusion = f32[16896]{0:T(1024)S(1)} fusion(bf16[16896,256]{1,0:T(8,128)(2,1)} %all-gather.2.cloned.1.call-done), kind=kLoop, calls=%fused_computation.1 | loop fusion | flops 12959232 | bytes 8718336 | tf_op jit(solution)/shard_map/reduce_sum | solution.py:8
  158.0 0.3 copy-done
  158.3 5.4 %subtract_reduce_fusion = f32[512]{0:T(512)S(1)} fusion(bf16[512,256]{1,0:T(8,128)(2,1)S(1)} %all_gather.7, bf16[16896,256]{1,0:T(8,128)(2,1)S(1)} %copy-done, f32[16896]{0:T(1024)S(1)} %multiply_reduce_fusion), kind=kOutput, calls=%fused_computation | convolution fusion | flops 4455136768 | bytes 8982528 | tf_op jit(solution)/shard_map/dot_general | solution.py:9
  163.7 0.0 copy-done.1
  163.7 16.4 %pmin.7 = f32[512]{0:T(512)S(1)} all-reduce(f32[512]{0:T(512)S(1)} %subtract_reduce_fusion), channel_id=1, replica_groups=mesh['blk'=96,'grp'=8] {'grp'}, use_global_device_ids=true, to_apply=%region_3.0 | all-reduce | flops 512 | bytes 4096 | tf_op jit(solution)/shard_map/pmin | solution.py:28
  180.1 0.6 add_multiply_fusion
  (2 shorter events, 0.0 us)
Async XLA Ops:
  7.2 145.0 %all-gather.2.cloned.1.call-start = ((), (), s32[]{:S(2)}) async-start(), calls=%async_computation.2 | async-start | bytes 8740864 | tf_op jit(solution)/shard_map/all_gather | solution.py:26
  12.0 30.1 %all-to-all-start = ((bf16[8,1,32]{2,1,0:T(2,128)(2,1)}), bf16[8,1,32]{2,1,0:T(2,128)(2,1)S(1)}, u32[]{:S(2)}, u32[]{:S(2)}) async-start(bf16[8,1,32]{2,1,0:T(2,128)(2,1)} %convert_element_type.71), calls=%async_computation | async-start | bytes 8192 | tf_op jit(solution)/shard_map/all_to_all | solution.py:53
  42.1 9.1 %all-to-all-start.1 = ((bf16[8,32,256]{2,1,0:T(8,128)(2,1)}), bf16[8,32,256]{2,1,0:T(8,128)(2,1)S(1)}, u32[]{:S(2)}, u32[]{:S(2)}) async-start(bf16[8,32,256]{2,1,0:T(8,128)(2,1)} %bitcast.2), calls=%async_computation.1 | async-start | bytes 262144 | tf_op jit(solution)/shard_map/all_to_all | solution.py:50
  46.8 116.8 %copy-start.1 = (f32[176]{0:T(256)}, f32[176]{0:T(256)S(1)}, u32[]{:S(2)}) copy-start(f32[176]{0:T(256)S(1)} %add.26) | copy-start | bytes 2116
  152.2 6.1 %copy-start = (bf16[16896,256]{1,0:T(8,128)(2,1)S(1)}, bf16[16896,256]{1,0:T(8,128)(2,1)}, u32[]{:S(2)}) copy-start(bf16[16896,256]{1,0:T(8,128)(2,1)} %all-gather.2.cloned.1.call-done) | copy-start | bytes 25952260
Sparse Core Ops, SparseCore 0:
  11.7 140.4 all-gather.1
where the time goes:
time: 188 us
  waiting for transfers between devices  104 us (55%)
  blocking collectives  30 us (16%)
  starting transfers between devices  17.6 us (9%)
  between operations  14.1 us (8%)
  other arithmetic  11.5 us (6%)
  matrix products  9.75 us (5%)
    all_gather x1, waiting for transfers between devices, on_device(): lax.all_gather(centroids_low, 'blk', axis=0, tiled=True)  99.2 us
    pmin x1, blocking collectives, on_device(): combined = lax.pmin(partial_value, 'grp')  16.4 us
    all_to_all x1, starting transfers between devices, on_device(): lax.all_to_all(slot_cell.reshape(groups, capacity).astype(jnp.bfloat16),...  13.7 us
    all_gather x1, blocking collectives, on_device(): gathered = lax.all_gather(points_low, 'grp', axis=0, tiled=True)  13.5 us
    reduce_sum x1, other arithmetic, nearest_fold(): row_norms = jnp.sum(jnp.square(portion.astype(jnp.float32)), axis=1)  5.77 us
    dot_general x1, matrix products, nearest_fold(): lax.dot_general(rows_low, portion, (((1,), (1,)), ((), ())), preferred_el...  5.42 us
    all_to_all x1, waiting for transfers between devices, on_device(): lax.all_to_all(outgoing.astype(jnp.bfloat16), 'grp', split_axis=0, concat...  4.37 us
    all_to_all x1, starting transfers between devices, on_device(): lax.all_to_all(outgoing.astype(jnp.bfloat16), 'grp', split_axis=0, concat...  3.83 us
  transfers between devices with their start and end apart: 3, of which 2 were waited for; matrix products, arithmetic and copies ran while one was open for 5% of the time, Pallas kernels for 0%

commit v1 on v0

v1 whole, which is shorter than its diff:
```python
import jax
import jax.numpy as jnp
from jax import lax
from jax.sharding import PartitionSpec as P


def on_device(points, centroids, counts, assign):
    pts_rows = points.shape[0]
    feature_width = points.shape[1]
    cen_rows = centroids.shape[0]
    blocks = lax.axis_size("blk")
    points_low = points.astype(jnp.bfloat16)
    centroids_low = centroids.astype(jnp.bfloat16)
    point_norms = jnp.sum(points * points, axis=1)
    cen_norms = jnp.sum(jnp.square(centroids_low.astype(jnp.float32)), axis=1)

    all_points = lax.all_gather(points_low, "blk", axis=0, tiled=True)
    cell_low = lax.all_gather(centroids_low, "grp", axis=0, tiled=True)
    cell_norms = lax.all_gather(cen_norms, "grp", axis=0, tiled=True)
    scores = lax.dot_general(
        all_points, cell_low, (((1,), (1,)), ((), ())), preferred_element_type=jnp.float32
    )
    partial_value = jnp.min(cell_norms[None, :] - 2.0 * scores, axis=1)
    exchanged = lax.all_to_all(
        partial_value.reshape(blocks, pts_rows), "blk", split_axis=0, concat_axis=0, tiled=True
    )
    own_rows = jnp.min(exchanged, axis=0)
    nearest = (point_norms + own_rows) / feature_width

    cell_points = lax.all_gather(points_low, "grp", axis=0, tiled=True)
    cell_assign = lax.all_gather(assign, "grp", axis=0, tiled=True)
    local_index = cell_assign - lax.axis_index("grp") * cen_rows
    matches = local_index[None, :] == jnp.arange(cen_rows, dtype=jnp.int32)[:, None]
    totals = jnp.dot(
        matches.astype(jnp.bfloat16), cell_points, preferred_element_type=jnp.float32
    )
    arrivals = jnp.sum(matches.astype(jnp.float32), axis=1)
    new_counts = counts + arrivals
    new_centroids = (counts[:, None] * centroids + totals) / new_counts[:, None]
    return (nearest, new_centroids, new_counts)


def solution(mesh):
    return jax.shard_map(
        on_device,
        mesh=mesh,
        in_specs=(
            P(("blk", "grp"), None),
            P(("blk", "grp"), None),
            P(("blk", "grp")),
            P(("blk", "grp")),
        ),
        out_specs=(P(("blk", "grp")), P(("blk", "grp"), None), P(("blk", "grp"))),
        check_vma=False,
    )
```

time: 188 us -> 185 us (0.984)
  the two profiles are of different devices: /device:TPU:1 before, /device:TPU:2 now
where the time goes in v1:
time: 185 us
  waiting for transfers between devices  88.9 us (48%)
  blocking collectives  53.6 us (29%)
  between operations  15.4 us (8%)
  starting transfers between devices  12 us (6%)
  matrix products  7.76 us (4%)
  other arithmetic  4.12 us (2%)
  local copies, waits for them, and re-layouts  3.12 us (2%)
    all_gather x1, waiting for transfers between devices, on_device(): all_points = lax.all_gather(points_low, 'blk', axis=0, tiled=True)  75.6 us
    unnamed x2, blocking collectives  26.2 us
    all_gather x1, blocking collectives, on_device(): cell_points = lax.all_gather(points_low, 'grp', axis=0, tiled=True)  13.8 us
    all_gather x1, blocking collectives, on_device(): cell_low = lax.all_gather(centroids_low, 'grp', axis=0, tiled=True)  13.6 us
    all_to_all x1, waiting for transfers between devices, on_device(): lax.all_to_all(partial_value.reshape(blocks, pts_rows), 'blk', split_axis...  13.3 us
    all_to_all x1, starting transfers between devices, on_device(): lax.all_to_all(partial_value.reshape(blocks, pts_rows), 'blk', split_axis...  11.9 us
    dot_general x1, matrix products, on_device(): lax.dot_general(all_points, cell_low, (((1,), (1,)), ((), ())), preferred...  6.87 us
  transfers between devices with their start and end apart: 2, of which 2 were waited for; matrix products, arithmetic and copies ran while one was open for 3% of the time, Pallas kernels for 0%

profile of v1, /device:TPU:2, one launch (start us, length us, event | category | flops | bytes accessed | tf_op | source)
XLA Modules:
  0.0 184.9 jit_solution(17986256279121466053)
XLA Ops:
  7.2 0.0 all-gather.2.cloned.1.call-start
  7.2 1.6 fusion.2
  8.9 0.0 all-gather.2.cloned.1.call-update
  8.9 1.3 dynamic-slice
  11.5 0.9 dynamic-update-slice.1
  12.3 14.3 %all-reduce.1 = s32[512]{0:T(512)S(1)} all-reduce(s32[512]{0:T(512)S(1)} %dynamic-update-slice.1), channel_id=1, replica_groups=mesh['blk'=96,'grp'=8] {'grp'}, use_global_device_ids=true, to_apply=%add.1 | all-reduce | flops 512 | bytes 4096
  26.6 0.1 convert_reduce_fusion
  26.8 0.7 add.11
  27.4 0.0 copy-start.2
  27.4 1.0 multiply_reduce_fusion
  28.5 0.3 dynamic-update-slice
  28.8 12.0 %all-reduce = f32[1408]{0:T(1024)S(1)} all-reduce(f32[1408]{0:T(1024)S(1)} %dynamic-update-slice), channel_id=1, replica_groups=mesh['blk'=96,'grp'=8] {'grp'}, use_global_device_ids=true, to_apply=%add | all-reduce | flops 1408 | bytes 11264
  40.7 13.8 %all_gather.19 = bf16[512,256]{1,0:T(8,128)(2,1)S(1)} all-gather(bf16[64,256]{1,0:T(8,128)(2,1)} %get-tuple-element.5), channel_id=1, replica_groups=mesh['blk'=96,'grp'=8] {'grp'}, dimensions={0}, use_global_device_ids=true | all-gather | bytes 294912 | tf_op jit(solution)/shard_map/all_gather | solution.py:30
  54.6 13.6 %all_gather.17 = bf16[1408,256]{1,0:T(8,128)(2,1)S(1)} all-gather(bf16[176,256]{1,0:T(8,128)(2,1)S(1)} %get-tuple-element.4), channel_id=1, replica_groups=mesh['blk'=96,'grp'=8] {'grp'}, dimensions={0}, use_global_device_ids=true | all-gather | bytes 811008 | tf_op jit(solution)/shard_map/all_gather | solution.py:18
  68.1 0.0 copy-start
  68.1 0.0 copy-start.1
  68.1 75.6 %all-gather.2.cloned.1.call-done = bf16[6144,256]{1,0:T(8,128)(2,1)} async-done(((bf16[64,256]{1,0:T(8,128)(2,1)}), bf16[6144,256]{1,0:T(8,128)(2,1)}) %all-gather.2.cloned.1.call-update) | async-done | bytes 3145744 | tf_op jit(solution)/shard_map/all_gather | solution.py:17
  143.7 6.9 %subtract_reduce_fusion = f32[6144]{0:T(1024)S(1)} fusion(bf16[6144,256]{1,0:T(8,128)(2,1)} %all-gather.2.cloned.1.call-done, bf16[1408,256]{1,0:T(8,128)(2,1)S(1)} %all_gather.17, f32[1408]{0:T(1024)S(1)} %all-reduce), kind=kOutput, calls=%fused_computation | convolution fusion | flops 4455131136 | bytes 3896832 | tf_op jit(solution)/shard_map/dot_general | solution.py:20
  150.6 0.7 all_to_all.6
  151.3 11.9 %all-to-all-start = ((f32[96,1,64]{2,1,0:T(1,128)}), f32[96,1,64]{2,1,0:T(1,128)S(1)}, u32[]{:S(2)}, u32[]{:S(2)}) async-start(f32[96,1,64]{2,1,0:T(1,128)} %bitcast.1), calls=%async_computation | async-start | bytes 98304 | tf_op jit(solution)/shard_map/all_to_all | solution.py:24
  163.2 0.0 copy-done.2
  163.2 0.0 copy-done
  163.3 0.0 copy-done.1
  163.3 0.9 fusion
  164.2 13.3 %all-to-all-done = f32[96,1,64]{2,1,0:T(1,128)S(1)} async-done(((f32[96,1,64]{2,1,0:T(1,128)}), f32[96,1,64]{2,1,0:T(1,128)S(1)}, u32[]{:S(2)}, u32[]{:S(2)}) %all-to-all-start) | async-done | bytes 24608 | tf_op jit(solution)/shard_map/all_to_all | solution.py:24
  177.4 0.1 reduce_min.19
  177.5 0.5 add_multiply_fusion
  (3 shorter events, 0.0 us)
Async XLA Ops:
  7.2 136.6 %all-gather.2.cloned.1.call-start = ((), (), s32[]{:S(2)}) async-start(), calls=%async_computation.1 | async-start | bytes 3178496 | tf_op jit(solution)/shard_map/all_gather | solution.py:17
  27.4 135.8 %copy-start.2 = (f32[176]{0:T(256)}, f32[176]{0:T(256)S(1)}, u32[]{:S(2)}) copy-start(f32[176]{0:T(256)S(1)} %add.11) | copy-start | bytes 2116
  68.1 95.1 %copy-start = (f32[176,256]{1,0:T(8,128)S(1)}, f32[176,256]{1,0:T(8,128)}, u32[]{:S(2)}) copy-start(f32[176,256]{1,0:T(8,128)} %param.5) | copy-start | bytes 540676
  68.1 95.1 %copy-start.1 = (f32[176]{0:T(256)S(1)}, f32[176]{0:T(256)}, u32[]{:S(2)}) copy-start(f32[176]{0:T(256)} %param.6) | copy-start | bytes 2116
  151.3 26.1 %all-to-all-start = ((f32[96,1,64]{2,1,0:T(1,128)}), f32[96,1,64]{2,1,0:T(1,128)S(1)}, u32[]{:S(2)}, u32[]{:S(2)}) async-start(f32[96,1,64]{2,1,0:T(1,128)} %bitcast.1), calls=%async_computation | async-start | bytes 98304 | tf_op jit(solution)/shard_map/all_to_all | solution.py:24
Sparse Core Ops, SparseCore 0:
  12.3 131.3 all-gather.1

commit v2 on v1

v2 whole, which is shorter than its diff:
```python
import jax
import jax.numpy as jnp
import numpy as np
from jax import lax
from jax.sharding import Mesh
from jax.sharding import PartitionSpec as P

PT_GATHER = "split"
GRP_GATHER = "xla"
MIN_EX = "a2a"
AXES = ("y", "z", "x", "c")
ALL = AXES


def gather_grp(block):
    if GRP_GATHER == "xla":
        return lax.all_gather(block, ("x", "c"), axis=0, tiled=False)
    n = lax.axis_size(("x", "c"))
    me = lax.axis_index(("x", "c"))
    pieces = [block]
    for k in range(1, n):
        perm = [(j, (j + k) % n) for j in range(n)]
        pieces.append(lax.ppermute(block, ("x", "c"), perm))
    stacked = jnp.stack(pieces)
    order = (me - jnp.arange(n)) % n
    inv = jnp.zeros((n,), jnp.int32).at[order].set(jnp.arange(n, dtype=jnp.int32))
    return jnp.take(stacked, inv, axis=0)


def on_device(points, centroids, counts, assign):
    pts_rows, feature_width = points.shape
    cen_rows = centroids.shape[0]
    n_y = lax.axis_size("y")
    n_z = lax.axis_size("z")
    points_low = points.astype(jnp.bfloat16)
    centroids_low = centroids.astype(jnp.bfloat16)
    point_norms = jnp.sum(points * points, axis=1)

    if PT_GATHER == "split":
        all_points = lax.all_gather(lax.all_gather(points_low, "z", axis=0, tiled=True), "y", axis=0, tiled=True)
    else:
        all_points = lax.all_gather(points_low, ("y", "z"), axis=0, tiled=True)

    hi = (assign // 64).astype(jnp.bfloat16)
    lo = (assign % 64).astype(jnp.bfloat16)
    code = jnp.concatenate([hi, lo, jnp.zeros((feature_width - 2 * pts_rows,), jnp.bfloat16)])[None, :]
    block = jnp.concatenate([centroids_low, points_low, code], axis=0)
    grp_all = gather_grp(block)
    n_grp = grp_all.shape[0]
    cell_low = grp_all[:, :cen_rows].reshape(n_grp * cen_rows, feature_width)
    cell_points = grp_all[:, cen_rows:cen_rows + pts_rows].reshape(n_grp * pts_rows, feature_width)
    codes = grp_all[:, cen_rows + pts_rows].astype(jnp.int32)
    cell_assign = (codes[:, :pts_rows] * 64 + codes[:, pts_rows:2 * pts_rows]).reshape(-1)
    cell_norms = jnp.sum(jnp.square(cell_low.astype(jnp.float32)), axis=1)

    scores = lax.dot_general(all_points, cell_low, (((1,), (1,)), ((), ())), preferred_element_type=jnp.float32)
    partial_value = jnp.min(cell_norms[None, :] - 2.0 * scores, axis=1)
    if MIN_EX == "a2a2":
        pv = partial_value.reshape(n_y, n_z, pts_rows)
        s1 = lax.all_to_all(pv, "z", split_axis=1, concat_axis=1, tiled=True)
        m1 = jnp.min(s1, axis=1)
        s2 = lax.all_to_all(m1, "y", split_axis=0, concat_axis=0, tiled=True)
        own_rows = jnp.min(s2, axis=0)
    elif MIN_EX == "a2a":
        s = lax.all_to_all(partial_value.reshape(n_y * n_z, pts_rows), ("y", "z"), split_axis=0, concat_axis=0, tiled=True)
        own_rows = jnp.min(s, axis=0)
    else:
        full = lax.pmin(partial_value, ("y", "z"))
        own_rows = lax.dynamic_slice_in_dim(full, lax.axis_index(("y", "z")) * pts_rows, pts_rows)
    nearest = (point_norms + own_rows) / feature_width

    local_index = cell_assign - lax.axis_index(("x", "c")) * cen_rows
    matches = local_index[None, :] == jnp.arange(cen_rows, dtype=jnp.int32)[:, None]
    totals = jnp.dot(matches.astype(jnp.bfloat16), cell_points, preferred_element_type=jnp.float32)
    arrivals = jnp.sum(matches.astype(jnp.float32), axis=1)
    new_counts = counts + arrivals
    new_centroids = (counts[:, None] * centroids + totals) / new_counts[:, None]
    return (nearest, new_centroids, new_counts)


def solution(mesh):
    devs = np.asarray(mesh.devices)
    flat = devs.reshape(-1)
    n_y = len({d.coords[1] for d in flat})
    n_z = len({d.coords[2] for d in flat})
    n_x = len({d.coords[0] for d in flat})
    split = Mesh(devs.reshape(n_y, n_z, n_x, flat.size // (n_y * n_z * n_x)), AXES)
    row = P(ALL, None)
    vec = P(ALL)
    return jax.shard_map(on_device, mesh=split, in_specs=(row, row, vec, vec), out_specs=(vec, row, vec), check_vma=False)
```

time: 185 us -> 133 us (0.72)
  the two profiles are of different devices: /device:TPU:2 before, /device:TPU:1 now
where the time goes in v2:
time: 133 us
  blocking collectives  51.8 us (39%)
  waiting for transfers between devices  39.3 us (30%)
  starting transfers between devices  14.6 us (11%)
  between operations  14.2 us (11%)
  matrix products  7.82 us (6%)
  other arithmetic  3.91 us (3%)
    all_gather x1, blocking collectives, on_device(): lax.all_gather(points_low, 'z', axis=0, tiled=True)  31.5 us
    all_gather x1, waiting for transfers between devices, on_device(): lax.all_gather(lax.all_gather(points_low, 'z', axis=0, tiled=True), 'y',...  27.1 us
    all_gather x1, blocking collectives, gather_grp(): return lax.all_gather(block, ('x', 'c'), axis=0, tiled=False)  20.4 us
    all_to_all x1, starting transfers between devices, on_device(): lax.all_to_all(partial_value.reshape(n_y * n_z, pts_rows), ('y', 'z'), sp...  14.6 us
    all_to_all x1, waiting for transfers between devices, on_device(): lax.all_to_all(partial_value.reshape(n_y * n_z, pts_rows), ('y', 'z'), sp...  12.1 us
    dot_general x1, matrix products, on_device(): lax.dot_general(all_points, cell_low, (((1,), (1,)), ((), ())), preferred...  6.93 us
  transfers between devices with their start and end apart: 2, of which 2 were waited for; matrix products, arithmetic and copies ran while one was open for 3% of the time, Pallas kernels for 0%

profile of v2, /device:TPU:1, one launch (start us, length us, event | category | flops | bytes accessed | tf_op | source)
XLA Modules:
  0.0 132.5 jit_solution(11203905122132644384)
XLA Ops:
  7.2 0.0 copy-start.1
  7.2 0.0 all-gather.4.cloned.1.call-start
  7.2 1.0 fusion.5
  8.2 31.5 %all_gather.14 = bf16[768,256]{1,0:T(8,128)(2,1)} all-gather(bf16[64,256]{1,0:T(8,128)(2,1)S(1)} %get-tuple-element.3), channel_id=1, replica_groups=mesh['y'=8,'z'=12,'x'=4,'c'=2] {'z'}, dimensions={0}, use_global_device_ids=true | all-gather | bytes 425984 | tf_op jit(solution)/shard_map/all_gather | solution.py:40
  39.7 0.0 all-gather.4.cloned.1.call-update
  39.8 0.7 fusion.4
  40.4 0.1 pad_maximum_fusion
  40.5 0.9 convert_element_type.26
  41.5 20.4 %all-gather.1 = bf16[8,241,256]{2,1,0:T(8,128)(2,1)S(1)} all-gather(bf16[1,241,256]{2,1,0:T(8,128)(2,1)S(1)} %maximum_bitcast_fusion), channel_id=2, replica_groups=mesh['y'=8,'z'=12,'x'=4,'c'=2] {'x','c'}, dimensions={0}, use_global_device_ids=true | all-gather | bytes 1110528 | tf_op jit(solution)/shard_map/all_gather | solution.py:17
  61.9 0.1 fusion.2
  62.0 0.1 sub.36
  62.1 0.4 multiply_reduce_fusion
  62.4 0.1 sub.31
  62.5 0.1 convert_reduce_fusion
  62.7 0.0 copy-done.1
  62.7 0.0 copy-start.2
  62.7 27.1 %all-gather.4.cloned.1.call-done = bf16[6144,256]{1,0:T(8,128)(2,1)} async-done(((bf16[768,256]{1,0:T(8,128)(2,1)}), bf16[6144,256]{1,0:T(8,128)(2,1)}) %all-gather.4.cloned.1.call-update) | async-done | bytes 3145744 | tf_op jit(solution)/shard_map/all_gather | solution.py:40
  89.8 0.0 copy-start
  89.8 6.9 %subtract_reduce_fusion = f32[6144]{0:T(1024)S(1)} fusion(bf16[1408,256]{1,0:T(8,128)(2,1)S(1)} %bitcast.11, bf16[6144,256]{1,0:T(8,128)(2,1)} %all-gather.4.cloned.1.call-done, f32[1408]{0:T(1024)S(1)} %sub.31), kind=kOutput, calls=%fused_computation | convolution fusion | flops 4455131136 | bytes 3896832 | tf_op jit(solution)/shard_map/dot_general | solution.py:56
  96.7 0.7 all_to_all.6
  97.4 14.6 %all-to-all-start = ((f32[96,1,64]{2,1,0:T(1,128)}), f32[96,1,64]{2,1,0:T(1,128)S(1)}, u32[]{:S(2)}, u32[]{:S(2)}) async-start(f32[96,1,64]{2,1,0:T(1,128)} %bitcast.2), calls=%async_computation | async-start | bytes 98304 | tf_op jit(solution)/shard_map/all_to_all | solution.py:65
  112.0 0.0 copy-done.2
  112.0 0.0 copy-done
  112.0 0.9 fusion
  112.9 12.1 %all-to-all-done = f32[96,1,64]{2,1,0:T(1,128)S(1)} async-done(((f32[96,1,64]{2,1,0:T(1,128)}), f32[96,1,64]{2,1,0:T(1,128)S(1)}, u32[]{:S(2)}, u32[]{:S(2)}) %all-to-all-start) | async-done | bytes 24608 | tf_op jit(solution)/shard_map/all_to_all | solution.py:65
  125.1 0.1 reduce_min.19
  125.2 0.5 add_multiply_fusion
  (8 shorter events, 0.1 us)
Async XLA Ops:
  7.2 55.5 %copy-start.1 = (f32[176]{0:T(256)S(1)}, f32[176]{0:T(256)}, u32[]{:S(2)}) copy-start(f32[176]{0:T(256)} %param.6) | copy-start | bytes 2116
  7.2 82.6 %all-gather.4.cloned.1.call-start = ((), (), s32[]{:S(2)}) async-start(), calls=%async_computation.1 | async-start | bytes 3538944 | tf_op jit(solution)/shard_map/all_gather | solution.py:40
  62.7 49.3 %copy-start.2 = (f32[176]{0:T(256)}, f32[176]{0:T(256)S(1)}, u32[]{:S(2)}) copy-start(f32[176]{0:T(256)S(1)} %add.27) | copy-start | bytes 2116
  89.8 22.2 %copy-start = (f32[176,256]{1,0:T(8,128)S(1)}, f32[176,256]{1,0:T(8,128)}, u32[]{:S(2)}) copy-start(f32[176,256]{1,0:T(8,128)} %param.5) | copy-start | bytes 540676
  97.4 27.6 %all-to-all-start = ((f32[96,1,64]{2,1,0:T(1,128)}), f32[96,1,64]{2,1,0:T(1,128)S(1)}, u32[]{:S(2)}, u32[]{:S(2)}) async-start(f32[96,1,64]{2,1,0:T(1,128)} %bitcast.2), calls=%async_computation | async-start | bytes 98304 | tf_op jit(solution)/shard_map/all_to_all | solution.py:65
Sparse Core Ops, SparseCore 0:
  39.9 49.8 all-gather.3

commit v3 on v1

v3 whole, which is shorter than its diff:
```python
import jax
import jax.numpy as jnp
import numpy as np
from jax import lax
from jax.sharding import Mesh
from jax.sharding import PartitionSpec as P

AXES = ("y", "z", "x", "c")
STAGES = ("z", ("x", "c"))


def on_device(points, centroids, counts, assign):
    pts_rows, feature_width = points.shape
    cen_rows = centroids.shape[0]
    sizes = {a: lax.axis_size(a) for a in ("z", "x", "c")}
    points_low = points.astype(jnp.bfloat16)
    centroids_low = centroids.astype(jnp.bfloat16)
    point_norms = jnp.sum(points * points, axis=1)

    all_points = points_low
    for axis in STAGES:
        all_points = lax.all_gather(all_points, axis, axis=0, tiled=True)
    order = tuple(a for axis in reversed(STAGES) for a in ((axis,) if isinstance(axis, str) else axis))
    slice_low = lax.all_gather(centroids_low, "y", axis=0, tiled=True)
    slice_norms = jnp.sum(jnp.square(slice_low.astype(jnp.float32)), axis=1)

    scores = lax.dot_general(all_points, slice_low, (((1,), (1,)), ((), ())), preferred_element_type=jnp.float32)
    partial_value = jnp.min(slice_norms[None, :] - 2.0 * scores, axis=1)
    shaped = partial_value.reshape(tuple(sizes[a] for a in order) + (pts_rows,))
    perm = tuple(order.index(a) for a in ("z", "x", "c")) + (len(order),)
    rows = shaped.transpose(perm).reshape(-1, pts_rows)
    exchanged = lax.all_to_all(rows, ("z", "x", "c"), split_axis=0, concat_axis=0, tiled=True)
    own_rows = jnp.min(exchanged, axis=0)
    nearest = (point_norms + own_rows) / feature_width

    mine = shaped.shape[:-1]
    cell = all_points.reshape(mine + (pts_rows, feature_width))
    cell = jnp.take(cell, lax.axis_index("z"), axis=order.index("z"))
    rest = tuple(a for a in order if a != "z")
    cell = cell.transpose(tuple(rest.index(a) for a in ("x", "c")) + (2, 3)).reshape(-1, feature_width)
    cell_assign = lax.all_gather(assign, ("x", "c"), axis=0, tiled=True)
    local_index = cell_assign - lax.axis_index(("x", "c")) * cen_rows
    matches = local_index[None, :] == jnp.arange(cen_rows, dtype=jnp.int32)[:, None]
    totals = jnp.dot(matches.astype(jnp.bfloat16), cell, preferred_element_type=jnp.float32)
    arrivals = jnp.sum(matches.astype(jnp.float32), axis=1)
    new_counts = counts + arrivals
    new_centroids = (counts[:, None] * centroids + totals) / new_counts[:, None]
    return (nearest, new_centroids, new_counts)


def solution(mesh):
    devs = np.asarray(mesh.devices)
    flat = devs.reshape(-1)
    n_y = len({d.coords[1] for d in flat})
    n_z = len({d.coords[2] for d in flat})
    n_x = len({d.coords[0] for d in flat})
    split = Mesh(devs.reshape(n_y, n_z, n_x, flat.size // (n_y * n_z * n_x)), AXES)
    row = P(AXES, None)
    vec = P(AXES)
    return jax.shard_map(on_device, mesh=split, in_specs=(row, row, vec, vec), out_specs=(vec, row, vec), check_vma=False)
```

time: 185 us -> 121 us (0.65)
  the two profiles are of different devices: /device:TPU:2 before, /device:TPU:1 now
where the time goes in v3:
time: 121 us; the launch traced here: 120 us
  blocking collectives  67.9 us (56%)
  between operations  14.8 us (12%)
  starting transfers between devices  11.9 us (10%)
  waiting for transfers between devices  10.5 us (9%)
  matrix products  7.78 us (6%)
  other arithmetic  4.68 us (4%)
  local copies, waits for them, and re-layouts  2.86 us (2%)
    all_gather x1, blocking collectives, on_device(): all_points = lax.all_gather(all_points, axis, axis=0, tiled=True)  31.5 us
    all_gather x1, blocking collectives, on_device(): slice_low = lax.all_gather(centroids_low, 'y', axis=0, tiled=True)  23.1 us
    unnamed x1, blocking collectives  13.3 us
    all_to_all x1, starting transfers between devices, on_device(): lax.all_to_all(rows, ('z', 'x', 'c'), split_axis=0, concat_axis=0, tiled=...  11.9 us
    all_to_all x1, waiting for transfers between devices, on_device(): lax.all_to_all(rows, ('z', 'x', 'c'), split_axis=0, concat_axis=0, tiled=...  10.5 us
    dot_general x1, matrix products, on_device(): lax.dot_general(all_points, slice_low, (((1,), (1,)), ((), ())), preferre...  6.89 us
  transfers between devices with their start and end apart: 2, of which 1 were waited for; matrix products, arithmetic and copies ran while one was open for 5% of the time, Pallas kernels for 0%

profile of v3, /device:TPU:1, one launch (start us, length us, event | category | flops | bytes accessed | tf_op | source)
XLA Modules:
  0.0 120.4 jit_solution(2680957962427597413)
XLA Ops:
  7.2 0.0 all-gather.2.cloned.1.call-start
  7.2 1.0 fusion.2
  8.2 31.5 %all_gather.13 = bf16[768,256]{1,0:T(8,128)(2,1)} all-gather(bf16[64,256]{1,0:T(8,128)(2,1)S(1)} %get-tuple-element.14), channel_id=1, replica_groups=mesh['y'=8,'z'=12,'x'=4,'c'=2] {'z'}, dimensions={0}, use_global_device_ids=true | all-gather | bytes 425984 | tf_op jit(solution)/shard_map/all_gather | solution.py:22
  39.7 0.0 all-gather.2.cloned.1.call-update
  39.7 0.9 convert_element_type.13
  40.7 1.3 %dynamic-slice.4 = u32[1]{0:T(128)} dynamic-slice(u32[768]{0:T(1024)} %constant.69, u32[]{:T(128)S(6)} %add.23), dynamic_slice_sizes={1} | dynamic-slice | bytes 12
  42.6 0.9 dynamic-update-slice.1
  43.5 13.3 %all-reduce = s32[512]{0:T(512)S(1)} all-reduce(s32[512]{0:T(512)S(1)} %dynamic-update-slice.1), channel_id=1, replica_groups=mesh['y'=8,'z'=12,'x'=4,'c'=2] {'x','c'}, use_global_device_ids=true, to_apply=%add | all-reduce | flops 512 | bytes 4096
  56.8 0.1 convert_reduce_fusion
  57.0 0.7 add.20
  57.6 0.0 copy-start.2
  57.6 23.1 %all_gather.12 = bf16[1408,256]{1,0:T(8,128)(2,1)S(1)} all-gather(bf16[176,256]{1,0:T(8,128)(2,1)S(1)} %convert_element_type.13), channel_id=1, replica_groups=mesh['y'=8,'z'=12,'x'=4,'c'=2] {'y'}, dimensions={0}, use_global_device_ids=true | all-gather | bytes 811008 | tf_op jit(solution)/shard_map/all_gather | solution.py:24
  80.7 0.3 multiply_reduce_fusion
  81.0 0.0 copy-start
  81.0 0.0 copy-start.1
  81.0 0.0 all-gather.2.cloned.1.call-done
  81.0 6.9 %subtract_reduce_fusion = f32[6144]{0:T(1024)S(1)} fusion(bf16[6144,256]{1,0:T(8,128)(2,1)} %all-gather.2.cloned.1.call-done, bf16[1408,256]{1,0:T(8,128)(2,1)S(1)} %all_gather.12, f32[1408]{0:T(1024)S(1)} %multiply_reduce_fusion), kind=kOutput, calls=%fused_computation | convolution fusion | flops 4455131136 | bytes 3896832 | tf_op jit(solution)/shard_map/dot_general | solution.py:27
  87.9 0.1 reshape.26
  88.0 0.6 copy.10
  88.7 11.9 %all-to-all-start = ((f32[96,1,64]{2,1,0:T(1,128)}), f32[96,1,64]{2,1,0:T(1,128)S(1)}, u32[]{:S(2)}, u32[]{:S(2)}) async-start(f32[96,1,64]{2,1,0:T(1,128)} %bitcast.2), calls=%async_computation | async-start | bytes 98304 | tf_op jit(solution)/shard_map/all_to_all | solution.py:32
  100.6 1.0 dynamic-slice_select_fusion
  101.6 0.0 copy-done.2
  101.6 0.0 copy-done
  101.6 0.0 copy-done.1
  101.6 0.9 fusion
  102.5 10.5 %all-to-all-done = f32[96,1,64]{2,1,0:T(1,128)S(1)} async-done(((f32[96,1,64]{2,1,0:T(1,128)}), f32[96,1,64]{2,1,0:T(1,128)S(1)}, u32[]{:S(2)}, u32[]{:S(2)}) %all-to-all-start) | async-done | bytes 24608 | tf_op jit(solution)/shard_map/all_to_all | solution.py:32
  113.0 0.1 reduce_min.19
  113.1 0.5 add_multiply_fusion
  (2 shorter events, 0.0 us)
Async XLA Ops:
  7.2 73.9 %all-gather.2.cloned.1.call-start = ((), (), s32[]{:S(2)}) async-start(), calls=%async_computation.1 | async-start | bytes 3538944 | tf_op jit(solution)/shard_map/all_gather | solution.py:22
  57.6 43.9 %copy-start.2 = (f32[176]{0:T(256)}, f32[176]{0:T(256)S(1)}, u32[]{:S(2)}) copy-start(f32[176]{0:T(256)S(1)} %add.20) | copy-start | bytes 2116
  81.0 20.6 %copy-start = (f32[176,256]{1,0:T(8,128)S(1)}, f32[176,256]{1,0:T(8,128)}, u32[]{:S(2)}) copy-start(f32[176,256]{1,0:T(8,128)} %param.5) | copy-start | bytes 540676
  81.0 20.6 %copy-start.1 = (f32[176]{0:T(256)S(1)}, f32[176]{0:T(256)}, u32[]{:S(2)}) copy-start(f32[176]{0:T(256)} %param.6) | copy-start | bytes 2116
  88.7 24.3 %all-to-all-start = ((f32[96,1,64]{2,1,0:T(1,128)}), f32[96,1,64]{2,1,0:T(1,128)S(1)}, u32[]{:S(2)}, u32[]{:S(2)}) async-start(f32[96,1,64]{2,1,0:T(1,128)} %bitcast.2), calls=%async_computation | async-start | bytes 98304 | tf_op jit(solution)/shard_map/all_to_all | solution.py:32
Sparse Core Ops, SparseCore 0:
  39.9 36.5 all-gather.1

commit v4 on v3

--- a/solution.py
+++ b/solution.py
@@ -7,6 +7,13 @@
 
 AXES = ("y", "z", "x", "c")
 STAGES = ("z", ("x", "c"))
+
+
+def gather_by_a2a(block, axis):
+    n = lax.axis_size(axis)
+    spread = jnp.broadcast_to(block[None], (n,) + block.shape)
+    got = lax.all_to_all(spread, axis, split_axis=0, concat_axis=0, tiled=True)
+    return got.reshape((n * block.shape[0],) + block.shape[1:])
 
 
 def on_device(points, centroids, counts, assign):
@@ -19,9 +26,12 @@
 
     all_points = points_low
     for axis in STAGES:
-        all_points = lax.all_gather(all_points, axis, axis=0, tiled=True)
+        if axis == "z":
+            all_points = gather_by_a2a(all_points, axis)
+        else:
+            all_points = lax.all_gather(all_points, axis, axis=0, tiled=True)
     order = tuple(a for axis in reversed(STAGES) for a in ((axis,) if isinstance(axis, str) else axis))
-    slice_low = lax.all_gather(centroids_low, "y", axis=0, tiled=True)
+    slice_low = gather_by_a2a(centroids_low, "y")
     slice_norms = jnp.sum(jnp.square(slice_low.astype(jnp.float32)), axis=1)
 
     scores = lax.dot_general(all_points, slice_low, (((1,), (1,)), ((), ())), preferred_element_type=jnp.float32)

time: 121 us -> 116 us (0.959)
  blocking collectives: 67.9 us -> 44.4 us
  waiting for transfers between devices: 10.5 us -> 21.6 us
  starting transfers between devices: 11.9 us -> 19.3 us
    all_gather x2 -> x0, blocking collectives: 54.5 us -> none  [the longest x1 31.5 us: on_device(): all_points = lax.all_gather(all_points, axis, axis=0, tiled=True)]
    all_to_all x0 -> x1, blocking collectives: none -> 34.3 us  [gather_by_a2a(): got = lax.all_to_all(spread, axis, split_axis=0, concat_axis=0, tiled=True)]
    all_to_all x0 -> x1, waiting for transfers between devices: none -> 7.48 us  [gather_by_a2a(): got = lax.all_to_all(spread, axis, split_axis=0, concat_axis=0, tiled=True)]
    all_to_all x0 -> x1, starting transfers between devices: none -> 6.82 us  [gather_by_a2a(): got = lax.all_to_all(spread, axis, split_axis=0, concat_axis=0, tiled=True)]
    all_gather x1, waiting for transfers between devices: 0.02 us -> 3.79 us  [on_device(): all_points = lax.all_gather(all_points, axis, axis=0, tiled=True)]
    unnamed x1, blocking collectives: 13.3 us -> 10.1 us
  transfers between devices with their start and end apart: 2 -> 3, of which waited for: 1 -> 3; matrix products, arithmetic and copies ran while one was open for 5% -> 5% of each run, Pallas kernels for 0% -> 0%
where the time goes in v4:
time: 116 us; the launch traced here: 115 us
  blocking collectives  44.4 us (38%)
  waiting for transfers between devices  21.6 us (19%)
  starting transfers between devices  19.3 us (17%)
  between operations  14.8 us (13%)
  matrix products  7.77 us (7%)
  other arithmetic  4.07 us (4%)
  local copies, waits for them, and re-layouts  3.29 us (3%)
    all_to_all x1, blocking collectives, gather_by_a2a(): got = lax.all_to_all(spread, axis, split_axis=0, concat_axis=0, tiled=True)  34.3 us
    all_to_all x1, starting transfers between devices, on_device(): lax.all_to_all(rows, ('z', 'x', 'c'), split_axis=0, concat_axis=0, tiled=...  12.5 us
    all_to_all x1, waiting for transfers between devices, on_device(): lax.all_to_all(rows, ('z', 'x', 'c'), split_axis=0, concat_axis=0, tiled=...  10.4 us
    unnamed x1, blocking collectives  10.1 us
    all_to_all x1, waiting for transfers between devices, gather_by_a2a(): got = lax.all_to_all(spread, axis, split_axis=0, concat_axis=0, tiled=True)  7.48 us
    dot_general x1, matrix products, on_device(): lax.dot_general(all_points, slice_low, (((1,), (1,)), ((), ())), preferre...  6.88 us
    all_to_all x1, starting transfers between devices, gather_by_a2a(): got = lax.all_to_all(spread, axis, split_axis=0, concat_axis=0, tiled=True)  6.82 us
    all_gather x1, waiting for transfers between devices, on_device(): all_points = lax.all_gather(all_points, axis, axis=0, tiled=True)  3.79 us
  transfers between devices with their start and end apart: 3, of which 3 were waited for; matrix products, arithmetic and copies ran while one was open for 5% of the time, Pallas kernels for 0%

profile of v4, /device:TPU:1, one launch (start us, length us, event | category | flops | bytes accessed | tf_op | source)
XLA Modules:
  0.0 115.3 jit_solution(11128748047209584123)
XLA Ops:
  7.2 0.0 copy-start.3
  7.2 0.0 copy-start.1
  7.2 0.0 all-gather.2.cloned.1.call-start
  7.2 1.0 fusion.2
  8.3 34.3 %all_to_all.19 = bf16[12,64,256]{2,1,0:T(8,128)(2,1)} all-to-all(bf16[12,64,256]{2,1,0:T(8,128)(2,1)S(1)} %broadcast_in_dim.17), channel_id=1, replica_groups=mesh['y'=8,'z'=12,'x'=4,'c'=2] {'z'}, dimensions={0} | all-to-all | bytes 786432 | tf_op jit(solution)/shard_map/all_to_all | solution.py:15
  42.6 0.0 all-gather.2.cloned.1.call-update
  42.6 0.9 convert_element_type.14
  43.6 0.9 broadcast_in_dim.16
  44.5 6.8 %all-to-all-start = ((bf16[8,176,256]{2,1,0:T(8,128)(2,1)}), bf16[8,176,256]{2,1,0:T(8,128)(2,1)S(1)}, u32[]{:S(2)}, u32[]{:S(2)}) async-start(bf16[8,176,256]{2,1,0:T(8,128)(2,1)} %broadcast_in_dim.16), calls=%async_computation | async-start | bytes 1441792 | tf_op jit(solution)/shard_map/all_to_all | solution.py:15
  51.3 1.3 %dynamic-slice.4 = u32[1]{0:T(128)} dynamic-slice(u32[768]{0:T(1024)} %constant.69, u32[]{:T(128)S(6)} %add.23), dynamic_slice_sizes={1} | dynamic-slice | bytes 12
  53.3 0.0 copy-done.3
  53.3 0.2 dynamic-update-slice.1
  53.5 10.1 %all-reduce = s32[512]{0:T(512)S(1)} all-reduce(s32[512]{0:T(512)S(1)} %dynamic-update-slice.1), channel_id=1, replica_groups=mesh['y'=8,'z'=12,'x'=4,'c'=2] {'x','c'}, use_global_device_ids=true, to_apply=%add | all-reduce | flops 512 | bytes 4096
  63.6 0.1 convert_reduce_fusion
  63.7 0.0 copy-done.1
  63.7 0.0 copy-start.2
  63.8 7.5 %all-to-all-done = bf16[8,176,256]{2,1,0:T(8,128)(2,1)S(1)} async-done(((bf16[8,176,256]{2,1,0:T(8,128)(2,1)}), bf16[8,176,256]{2,1,0:T(8,128)(2,1)S(1)}, u32[]{:S(2)}, u32[]{:S(2)}) %all-to-all-start) | async-done | bytes 720928 | tf_op jit(solution)/shard_map/all_to_all | solution.py:15
  71.2 0.4 multiply_reduce_fusion
  71.6 0.1 sub.16
  71.7 3.8 %all-gather.2.cloned.1.call-done = bf16[6144,256]{1,0:T(8,128)(2,1)} async-done(((bf16[768,256]{1,0:T(8,128)(2,1)}), bf16[6144,256]{1,0:T(8,128)(2,1)}) %all-gather.2.cloned.1.call-update) | async-done | bytes 3145744 | tf_op jit(solution)/shard_map/all_gather | solution.py:32
  75.5 0.0 copy-start
  75.5 6.9 %subtract_reduce_fusion = f32[6144]{0:T(1024)S(1)} fusion(bf16[6144,256]{1,0:T(8,128)(2,1)} %all-gather.2.cloned.1.call-done, bf16[1408,256]{1,0:T(8,128)(2,1)S(1)} %bitcast.12, f32[1408]{0:T(1024)S(1)} %sub.16), kind=kOutput, calls=%fused_computation | convolution fusion | flops 4455131136 | bytes 3896832 | tf_op jit(solution)/shard_map/dot_general | solution.py:37
  82.4 0.1 reshape.38
  82.4 0.6 copy.10
  83.1 12.5 %all-to-all-start.2 = ((f32[96,1,64]{2,1,0:T(1,128)}), f32[96,1,64]{2,1,0:T(1,128)S(1)}, u32[]{:S(2)}, u32[]{:S(2)}) async-start(f32[96,1,64]{2,1,0:T(1,128)} %bitcast.4), calls=%async_computation.2 | async-start | bytes 98304 | tf_op jit(solution)/shard_map/all_to_all | solution.py:42
  95.5 1.0 dynamic-slice_select_fusion
  96.5 0.0 copy-done.2
  96.5 0.0 copy-done
  96.5 0.9 fusion
  97.4 10.4 %all-to-all-done.2 = f32[96,1,64]{2,1,0:T(1,128)S(1)} async-done(((f32[96,1,64]{2,1,0:T(1,128)}), f32[96,1,64]{2,1,0:T(1,128)S(1)}, u32[]{:S(2)}, u32[]{:S(2)}) %all-to-all-start.2) | async-done | bytes 24608 | tf_op jit(solution)/shard_map/all_to_all | solution.py:42
  107.8 0.1 reduce_min.19
  107.9 0.5 add_multiply_fusion
  (4 shorter events, 0.1 us)
Async XLA Ops:
  7.2 46.1 %copy-start.3 = (s32[64]{0:T(128)S(1)}, s32[64]{0:T(128)}, u32[]{:S(2)}) copy-start(s32[64]{0:T(128)} %param.7) | copy-start | bytes 772
  7.2 56.5 %copy-start.1 = (f32[176]{0:T(256)S(1)}, f32[176]{0:T(256)}, u32[]{:S(2)}) copy-start(f32[176]{0:T(256)} %param.6) | copy-start | bytes 2116
  7.2 68.3 %all-gather.2.cloned.1.call-start = ((), (), s32[]{:S(2)}) async-start(), calls=%async_computation.3 | async-start | bytes 3538944 | tf_op jit(solution)/shard_map/all_gather | solution.py:32
  44.5 26.7 %all-to-all-start = ((bf16[8,176,256]{2,1,0:T(8,128)(2,1)}), bf16[8,176,256]{2,1,0:T(8,128)(2,1)S(1)}, u32[]{:S(2)}, u32[]{:S(2)}) async-start(bf16[8,176,256]{2,1,0:T(8,128)(2,1)} %broadcast_in_dim.16), calls=%async_computation | async-start | bytes 1441792 | tf_op jit(solution)/shard_map/all_to_all | solution.py:15
  63.7 32.8 %copy-start.2 = (f32[176]{0:T(256)}, f32[176]{0:T(256)S(1)}, u32[]{:S(2)}) copy-start(f32[176]{0:T(256)S(1)} %add.20) | copy-start | bytes 2116
  75.5 21.1 %copy-start = (f32[176,256]{1,0:T(8,128)S(1)}, f32[176,256]{1,0:T(8,128)}, u32[]{:S(2)}) copy-start(f32[176,256]{1,0:T(8,128)} %param.5) | copy-start | bytes 540676
  83.1 24.7 %all-to-all-start.2 = ((f32[96,1,64]{2,1,0:T(1,128)}), f32[96,1,64]{2,1,0:T(1,128)S(1)}, u32[]{:S(2)}, u32[]{:S(2)}) async-start(f32[96,1,64]{2,1,0:T(1,128)} %bitcast.4), calls=%async_computation.2 | async-start | bytes 98304 | tf_op jit(solution)/shard_map/all_to_all | solution.py:42
Sparse Core Ops, SparseCore 0:
  42.8 32.6 all-gather.1
